TPU v7x, 32 devices: a whole 2x2x4 slice. The times are simulated.
32 devices in a mesh: tm: 8 (over y, x, core), space: 4 (over z).
Axes of the slice: x: 2, y: 2, z: 4, core: 2. Of those that a mesh axis runs over, the one named last changes fastest.
Arguments:
- queries: bfloat16 [8, 4, 128, 1024], P('tm', 'space'), may hold values from -30 to 30
- key_vectors: bfloat16 [8, 4, 128, 1024], P('tm', 'space'), may hold values from -30 to 30
- value_vectors: bfloat16 [8, 4, 128, 1024], P('tm', 'space'), may hold values from -6 to 6
- key_blocks: int32 [8, 4, 2, 32], P('tm', 'space'), may hold values from 0 to 63, as said below
- block_count: int32 [8, 4, 2], P('tm', 'space'), may hold values from 1 to 32, as said below
Outputs:
- attention_out: bfloat16 [8, 4, 128, 1024], P('tm', 'space')
Inputs may be any that keep to these rules, and one draw needn't show every extreme that they name: `key_blocks`: A row's entries are distinct ids of blocks in the query block's own band or an adjacent one, of any frame group; its first entry is the query block itself. Only the first block_count entries of a list are used; on some devices a list uses all 32.
All inputs are finite; a program needn't handle non-finite values.
Results may differ from a plain program's by a relative error of at most 0.0044.
Values may be sent and summed in bfloat16 or wider, within the bound.
No kernel may reach another device: no remote copies, remote signals or barrier semaphores. Data moves between devices by JAX's collectives and lax.ppermute only.
A program may use at most 128 MiB of HBM per device.

v0:
```python
import jax
import jax.numpy as jnp
from jax import lax
from jax.sharding import PartitionSpec as P

HEADS = 8
HDIM = 128
BLOCK = 64
PICKS = 32


def with_halo(cells, sides, width):
    for axis, dim in sides:
        count = lax.axis_size(axis)
        ends = count - 1
        head = lax.slice_in_dim(cells, 0, width, axis=dim)
        tail = lax.slice_in_dim(cells, cells.shape[dim] - width, cells.shape[dim], axis=dim)
        cells = jnp.concatenate(
            [
                lax.ppermute(tail, axis, [(i, (i + 1) % count) for i in range(ends)]),
                cells,
                lax.ppermute(head, axis, [((i + 1) % count, i) for i in range(ends)]),
            ],
            axis=dim,
        )
    return cells


def on_device(queries, key_vectors, value_vectors, key_blocks, block_count):
    tokens_here = queries.shape[2]
    feature_width = queries.shape[3]
    blocks_here = tokens_here // BLOCK
    stacked = jnp.stack([key_vectors, value_vectors])
    banded = with_halo(stacked, (("space", 2),), 1)
    gathered = lax.all_gather(banded, "tm", axis=1, tiled=True)
    groups = gathered.shape[1]
    ordered = gathered.reshape(2, groups, 3, blocks_here, BLOCK, feature_width)
    tile_set = ordered.reshape(2, groups * 3 * blocks_here, BLOCK, feature_width)
    band_count = lax.axis_size("space")
    own_band = lax.axis_index("space")
    listed = key_blocks.reshape(blocks_here, PICKS)
    within = listed % blocks_here
    band_of = listed // blocks_here % band_count
    group_of = listed // (blocks_here * band_count)
    slots = (group_of * 3 + band_of - own_band + 1) * blocks_here + within
    chosen = tile_set[:, slots.reshape(-1)]
    keyset = chosen[0].reshape(blocks_here, PICKS * BLOCK, HEADS, HDIM)
    valset = chosen[1].reshape(blocks_here, PICKS * BLOCK, HEADS, HDIM)
    query_rows = queries.reshape(blocks_here, BLOCK, HEADS, HDIM)
    scores = jnp.einsum(
        "bqhd,bkhd->bhqk", query_rows, keyset, preferred_element_type=jnp.float32
    ) * HDIM ** (-0.5)
    usable = (jnp.arange(PICKS * BLOCK) // BLOCK)[None, :] < block_count.reshape(blocks_here, 1)
    scores = jnp.where(usable[:, None, None, :], scores, -1e30)
    peaks = jnp.max(scores, axis=-1, keepdims=True)
    weights = jnp.exp(scores - peaks)
    totals = jnp.sum(weights, axis=-1)
    rounded = weights.astype(jnp.bfloat16)
    blended = jnp.einsum("bhqk,bkhd->bqhd", rounded, valset, preferred_element_type=jnp.float32)
    result = blended / jnp.transpose(totals, (0, 2, 1))[:, :, :, None]
    return result.reshape(queries.shape).astype(jnp.bfloat16)


def solution(mesh):
    in_specs = (
        P("tm", "space", None, None),
        P("tm", "space", None, None),
        P("tm", "space", None, None),
        P("tm", "space", None, None),
        P("tm", "space", None),
    )
    out_specs = P("tm", "space", None, None)
    return jax.shard_map(
        on_device, mesh=mesh, in_specs=in_specs, out_specs=out_specs, check_vma=False
    )
```

profile of v0, /device:TPU:0, one launch (start us, length us, event | category | flops | bytes accessed | tf_op | source)
XLA Modules:
  0.0 168.3 jit_solution(12035285831225546549)
XLA Ops:
  6.5 0.0 all-gather.2.cloned.1.call-start
  6.5 1.1 pad_maximum_fusion.1
  7.6 5.0 %collective-permute-start = (bf16[2,1,1,128,1024]{4,3,2,1,0:T(8,128)(2,1)S(1)}, bf16[2,1,1,128,1024]{4,3,2,1,0:T(8,128)(2,1)S(1)}, u32[]{:S(2)}, u32[]{:S(2)}) collective-permute-start(bf16[2,1,1,128,1024]{4,3,2,1,0:T(8,128)(2,1)S(1)} %pad_maximum_fusion.1), channel_id=1, source_target_pairs={{0,1},{1,2},{2,3},{4,5},{5,6},{6,7},{8,9},{9,10},{10,11},{12,13},{... | collective-permute-start | bytes 1572872 | tf_op jit(solution)/shard_map/ppermute | solution.py:20
  12.6 1.3 collective-permute-start.1
  13.9 9.8 %collective-permute-done = bf16[2,1,1,128,1024]{4,3,2,1,0:T(8,128)(2,1)S(1)} collective-permute-done((bf16[2,1,1,128,1024]{4,3,2,1,0:T(8,128)(2,1)S(1)}, bf16[2,1,1,128,1024]{4,3,2,1,0:T(8,128)(2,1)S(1)}, u32[]{:S(2)}, u32[]{:S(2)}) %collective-permute-start) | collective-permute-done | bytes 524320 | tf_op jit(solution)/shard_map/ppermute | solution.py:20
  23.7 4.1 %collective-permute-done.1 = bf16[2,1,1,128,1024]{4,3,2,1,0:T(8,128)(2,1)S(1)} collective-permute-done((bf16[2,1,1,128,1024]{4,3,2,1,0:T(8,128)(2,1)S(1)}, bf16[2,1,1,128,1024]{4,3,2,1,0:T(8,128)(2,1)S(1)}, u32[]{:S(2)}, u32[]{:S(2)}) %collective-permute-start.1) | collective-permute-done | bytes 524320 | tf_op jit(solution)/shard_map/ppermute | solution.py:22
  27.9 2.4 %pad_maximum_fusion = bf16[2,1,3,128,1024]{4,3,2,1,0:T(8,128)(2,1)} fusion(bf16[2,1,1,128,1024]{4,3,2,1,0:T(8,128)(2,1)S(1)} %collective-permute-done.1, bf16[1,1,1,128,1024]{4,3,2,1,0:T(8,128)(2,1)} %bitcast.56, bf16[1,1,1,128,1024]{4,3,2,1,0:T(8,128)(2,1)} %bitcast.58, bf16[2,1,1,128,1024]{4,3,2,1,0:T(8,128)(2,1)S(1)} %collective-permute-done), kind=kLoop, calls=%fused_computation.15 | loop fusion | flops 2359296 | bytes 3145728 | tf_op jit(solution)/shard_map/concatenate | solution.py:18
  30.2 0.0 all-gather.2.cloned.1.call-update
  30.3 0.8 reshape.249
  31.0 1.0 copy.16
  32.1 0.7 broadcast_compare_fusion
  32.8 69.9 %all-gather.2.cloned.1.call-done = bf16[2,8,3,128,1024]{4,3,2,1,0:T(8,128)(2,1)} async-done(((bf16[2,1,3,128,1024]{4,3,2,1,0:T(8,128)(2,1)}), bf16[2,8,3,128,1024]{4,3,2,1,0:T(8,128)(2,1)}) %all-gather.2.cloned.1.call-update) | async-done | bytes 12582928 | tf_op jit(solution)/shard_map/all_gather | solution.py:35
  102.7 12.2 %gather_fusion = bf16[64,2,64,1024]{3,2,1,0:T(8,128)(2,1)} fusion(bf16[2,48,64,1024]{3,2,1,0:T(8,128)(2,1)} %bitcast.52, s32[1024]{0:T(1024)S(1)} %pad_clamp_fusion), kind=kCustom, calls=%fused_computation | custom fusion | bytes 33554688 | tf_op jit(solution)/shard_map/gather | solution.py:46
  114.9 12.1 %fusion.37 = (bf16[1,64,64,1024]{3,2,0,1:T(8,128)(2,1)}, bf16[1,64,64,1024]{3,2,0,1:T(8,128)(2,1)}) fusion(bf16[2,64,64,1024]{3,2,0,1:T(8,128)(2,1)} %bitcast.49), kind=kLoop, calls=%fused_computation.48 | loop fusion | bytes 33554432 | tf_op jit(solution)/shard_map/slice | solution.py:47
  127.1 8.8 %copy.15 = bf16[512,8,8,128]{3,2,1,0:T(8,128)(2,1)} copy(bf16[512,8,8,128]{3,1,2,0:T(8,128)(2,1)} %bitcast.51) | data formatting | bytes 16777216
  135.8 8.8 %copy.17 = bf16[512,8,8,128]{3,2,1,0:T(8,128)(2,1)} copy(bf16[512,8,8,128]{3,1,2,0:T(8,128)(2,1)} %bitcast.50) | data formatting | bytes 16777216
  144.6 7.2 %bitcast_reduce_fusion = (f32[2,8,64]{2,1,0:T(8,128)S(1)}, f32[2,8,2048,64]{2,3,1,0:T(8,128)S(1)}) fusion(pred[2,2048]{1,0:T(4,128)(4,1)S(1)} %broadcast_compare_fusion, bf16[2,64,8,128]{3,2,1,0:T(8,128)(2,1)S(1)} %bitcast.60, bf16[2,2048,8,128]{3,2,1,0:T(8,128)(2,1)} %bitcast.54), kind=kOutput, calls=%fused_computation.2 | convolution fusion | flops 543161344 | bytes 17047552 | tf_op jit(solution)/shard_map/bqhd,bkhd->bhqk/dot_general | solution.py:50
  151.8 2.1 %fusion.5 = f32[2,8,64]{2,1,0:T(8,128)S(1)} fusion(f32[2,8,2048,64]{2,3,1,0:T(8,128)S(1)} %get-tuple-element.8, f32[2,8,64]{2,1,0:T(8,128)S(1)} %get-tuple-element.7, pred[2,2048]{1,0:T(4,128)(4,1)S(1)} %broadcast_compare_fusion), kind=kLoop, calls=%fused_computation.9 | loop fusion | flops 8387584 | bytes 8400896 | tf_op jit(solution)/shard_map/reduce_sum | solution.py:57
  153.8 6.6 %fusion.22 = bf16[2,64,8,128]{3,1,2,0:T(8,128)(2,1)S(1)} fusion(bf16[2,2048,8,128]{3,2,1,0:T(8,128)(2,1)} %bitcast.53, f32[2,8,2048,64]{2,3,1,0:T(8,128)S(1)} %get-tuple-element.8, f32[2,8,64]{2,1,0:T(8,128)S(1)} %get-tuple-element.7, pred[2,2048]{1,0:T(4,128)(4,1)S(1)} %broadcast_compare_fusion, f32[2,64,8]{1,2,0:T(8,128)S(1)} %bitcast.61), kind=kOutput, calls=%fused_computation.18 | convolution fusion | flops 545521664 | bytes 17051648 | tf_op jit(solution)/shard_map/bhqk,bkhd->bqhd/dot_general | solution.py:59
  160.4 0.2 copy.14
  160.6 0.8 convert_element_type.19
  (3 shorter events, 0.0 us)
Async XLA Ops:
  6.5 96.2 %all-gather.2.cloned.1.call-start = ((), (), s32[]{:S(2)}) async-start(), calls=%async_computation | async-start | bytes 14155776 | tf_op jit(solution)/shard_map/all_gather | solution.py:35
  7.6 16.1 %collective-permute-start = (bf16[2,1,1,128,1024]{4,3,2,1,0:T(8,128)(2,1)S(1)}, bf16[2,1,1,128,1024]{4,3,2,1,0:T(8,128)(2,1)S(1)}, u32[]{:S(2)}, u32[]{:S(2)}) collective-permute-start(bf16[2,1,1,128,1024]{4,3,2,1,0:T(8,128)(2,1)S(1)} %pad_maximum_fusion.1), channel_id=1, source_target_pairs={{0,1},{1,2},{2,3},{4,5},{5,6},{6,7},{8,9},{9,10},{10,11},{12,13},{... | collective-permute-start | bytes 1572872 | tf_op jit(solution)/shard_map/ppermute | solution.py:20
  12.6 15.3 %collective-permute-start.1 = (bf16[2,1,1,128,1024]{4,3,2,1,0:T(8,128)(2,1)S(1)}, bf16[2,1,1,128,1024]{4,3,2,1,0:T(8,128)(2,1)S(1)}, u32[]{:S(2)}, u32[]{:S(2)}) collective-permute-start(bf16[2,1,1,128,1024]{4,3,2,1,0:T(8,128)(2,1)S(1)} %pad_maximum_fusion.1), channel_id=1, source_target_pairs={{1,0},{2,1},{3,2},{5,4},{6,5},{7,6},{9,8},{10,9},{11,10},{13,12},{... | collective-permute-start | bytes 1572872 | tf_op jit(solution)/shard_map/ppermute | solution.py:22
Sparse Core Ops, SparseCore 0:
  30.4 72.3 all-gather.1
where the time goes:
time: 169 us; the launch traced here: 168 us
  waiting for transfers between devices  83.9 us (50%)
  local copies, waits for them, and re-layouts  44.6 us (26%)
  matrix products  13.8 us (8%)
  between operations  13.5 us (8%)
  other arithmetic  6.27 us (4%)
  starting transfers between devices  6.25 us (4%)
    all_gather x1, waiting for transfers between devices, on_device(): gathered = lax.all_gather(banded, 'tm', axis=1, tiled=True)  69.9 us
    unnamed x3, local copies, waits for them, and re-layouts  18.5 us
    gather x1, local copies, waits for them, and re-layouts, on_device(): chosen = tile_set[:, slots.reshape(-1)]  12.2 us
    slice x1, local copies, waits for them, and re-layouts, on_device(): keyset = chosen[0].reshape(blocks_here, PICKS * BLOCK, HEADS, HDIM)  12.1 us
    ppermute x1, waiting for transfers between devices, with_halo(): lax.ppermute(tail, axis, [(i, (i + 1) % count) for i in range(ends)])  9.83 us
    dot_general x1, matrix products, on_device(): jnp.einsum('bqhd,bkhd->bhqk', query_rows, keyset, preferred_element_type=...  7.19 us
    dot_general x1, matrix products, on_device(): jnp.einsum('bhqk,bkhd->bqhd', rounded, valset, preferred_element_type=jnp...  6.57 us
    ppermute x1, starting transfers between devices, with_halo(): lax.ppermute(tail, axis, [(i, (i + 1) % count) for i in range(ends)])  4.96 us
  transfers between devices with their start and end apart: 3, of which 3 were waited for; matrix products, arithmetic and copies ran while one was open for 2% of the time, Pallas kernels for 0%

commit v1 on v0

--- a/solution.py
+++ b/solution.py
@@ -32,7 +32,15 @@
     blocks_here = tokens_here // BLOCK
     stacked = jnp.stack([key_vectors, value_vectors])
     banded = with_halo(stacked, (("space", 2),), 1)
-    gathered = lax.all_gather(banded, "tm", axis=1, tiled=True)
+    tmp, step_out, after = (lax.axis_size("tm"), lax.axis_index("tm"), banded.shape[1])
+    new, mixed_arr = (banded, 1)
+    while mixed_arr < tmp:
+        new = jnp.concatenate(
+            [new, lax.ppermute(new, "tm", tuple(((w, (w - mixed_arr) % tmp) for w in range(tmp))))],
+            1,
+        )
+        mixed_arr = 2 * mixed_arr
+    gathered = jnp.roll(new, step_out * after, 1)
     groups = gathered.shape[1]
     ordered = gathered.reshape(2, groups, 3, blocks_here, BLOCK, feature_width)
     tile_set = ordered.reshape(2, groups * 3 * blocks_here, BLOCK, feature_width)

time: 169 us -> 345 us (2.04)
  waiting for transfers between devices: 83.9 us -> 233 us
  local copies, waits for them, and re-layouts: 44.6 us -> 76.1 us
  between operations: 13.5 us -> 0.12 us
  other arithmetic: 6.27 us -> 12.8 us
    ppermute x0 -> x3, waiting for transfers between devices: none -> 219 us  [on_device(): lax.ppermute(new, 'tm', tuple(((w, (w - mixed_arr) % tmp) for w in range(...]
    all_gather x1 -> x0, waiting for transfers between devices: 69.9 us -> none  [on_device(): gathered = lax.all_gather(banded, 'tm', axis=1, tiled=True)]
    unnamed x3 -> x36, local copies, waits for them, and re-layouts: 18.5 us -> 33.5 us
    dynamic_slice x0 -> x1, local copies, waits for them, and re-layouts: none -> 10.6 us  [on_device(): gathered = jnp.roll(new, step_out * after, 1)]
    concatenate x0 -> x1, local copies, waits for them, and re-layouts: none -> 6.54 us  [on_device(): gathered = jnp.roll(new, step_out * after, 1)]
    concatenate x0 -> x2, other arithmetic: none -> 5.47 us  [on_device(): jnp.concatenate([new, lax.ppermute(new, 'tm', tuple(((w, (w - mixed_arr)...]
  transfers between devices with their start and end apart: 3 -> 5, of which waited for: 3 -> 5; matrix products, arithmetic and copies ran while one was open for 2% -> 2% of each run, Pallas kernels for 0% -> 0%
where the time goes in v1:
time: 345 us; the launch traced here: 344 us
  waiting for transfers between devices  233 us (68%)
  local copies, waits for them, and re-layouts  76.1 us (22%)
  matrix products  13.8 us (4%)
  other arithmetic  12.8 us (4%)
  starting transfers between devices  8.98 us (3%)
    ppermute x3, waiting for transfers between devices, on_device(): lax.ppermute(new, 'tm', tuple(((w, (w - mixed_arr) % tmp) for w in range(...  219 us
    unnamed x36, local copies, waits for them, and re-layouts  33.5 us
    gather x1, local copies, waits for them, and re-layouts, on_device(): chosen = tile_set[:, slots.reshape(-1)]  12.2 us
    slice x1, local copies, waits for them, and re-layouts, on_device(): keyset = chosen[0].reshape(blocks_here, PICKS * BLOCK, HEADS, HDIM)  12.2 us
    dynamic_slice x1, local copies, waits for them, and re-layouts, on_device(): gathered = jnp.roll(new, step_out * after, 1)  10.6 us
    ppermute x1, waiting for transfers between devices, with_halo(): lax.ppermute(tail, axis, [(i, (i + 1) % count) for i in range(ends)])  9.83 us
    dot_general x1, matrix products, on_device(): jnp.einsum('bqhd,bkhd->bhqk', query_rows, keyset, preferred_element_type=...  7.19 us
  transfers between devices with their start and end apart: 5, of which 5 were waited for; matrix products, arithmetic and copies ran while one was open for 2% of the time, Pallas kernels for 0%

profile of v1, /device:TPU:0, one launch (start us, length us, event | category | flops | bytes accessed | tf_op | source)
XLA Modules:
  0.0 344.4 jit_solution(17912533632691151019)
XLA Ops:
  1.2 5.0 %collective-permute-start = (bf16[2,1,1,128,1024]{4,3,2,1,0:T(8,128)(2,1)S(1)}, bf16[2,1,1,128,1024]{4,3,2,1,0:T(8,128)(2,1)S(1)}, u32[]{:S(2)}, u32[]{:S(2)}) collective-permute-start(bf16[2,1,1,128,1024]{4,3,2,1,0:T(8,128)(2,1)S(1)} %pad_maximum_fusion.6), channel_id=1, source_target_pairs={{0,1},{1,2},{2,3},{4,5},{5,6},{6,7},{8,9},{9,10},{10,11},{12,13},{... | collective-permute-start | bytes 1572872 | tf_op jit(solution)/shard_map/ppermute | solution.py:20
  6.1 1.3 collective-permute-start.1
  7.4 9.8 %collective-permute-done = bf16[2,1,1,128,1024]{4,3,2,1,0:T(8,128)(2,1)S(1)} collective-permute-done((bf16[2,1,1,128,1024]{4,3,2,1,0:T(8,128)(2,1)S(1)}, bf16[2,1,1,128,1024]{4,3,2,1,0:T(8,128)(2,1)S(1)}, u32[]{:S(2)}, u32[]{:S(2)}) %collective-permute-start) | collective-permute-done | bytes 524320 | tf_op jit(solution)/shard_map/ppermute | solution.py:20
  17.3 4.1 %collective-permute-done.1 = bf16[2,1,1,128,1024]{4,3,2,1,0:T(8,128)(2,1)S(1)} collective-permute-done((bf16[2,1,1,128,1024]{4,3,2,1,0:T(8,128)(2,1)S(1)}, bf16[2,1,1,128,1024]{4,3,2,1,0:T(8,128)(2,1)S(1)}, u32[]{:S(2)}, u32[]{:S(2)}) %collective-permute-start.1) | collective-permute-done | bytes 524320 | tf_op jit(solution)/shard_map/ppermute | solution.py:22
  21.4 2.7 pad_maximum_fusion.2
  24.8 17.9 %collective-permute-done.2 = bf16[2,1,3,128,1024]{4,3,2,1,0:T(8,128)(2,1)S(1)} collective-permute-done((bf16[2,1,3,128,1024]{4,3,2,1,0:T(8,128)(2,1)S(1)}, bf16[2,1,3,128,1024]{4,3,2,1,0:T(8,128)(2,1)S(1)}, u32[]{:S(2)}, u32[]{:S(2)}) %collective-permute-start.2) | collective-permute-done | bytes 1572896 | tf_op jit(solution)/shard_map/ppermute | solution.py:39
  42.8 1.8 pad_maximum_fusion.1
  44.6 1.8 collective-permute-start.3
  46.4 69.1 %collective-permute-done.3 = bf16[2,2,3,128,1024]{4,3,2,1,0:T(8,128)(2,1)S(1)} collective-permute-done((bf16[2,2,3,128,1024]{4,3,2,1,0:T(8,128)(2,1)S(1)}, bf16[2,2,3,128,1024]{4,3,2,1,0:T(8,128)(2,1)S(1)}, u32[]{:S(2)}, u32[]{:S(2)}) %collective-permute-start.3) | collective-permute-done | bytes 3145760 | tf_op jit(solution)/shard_map/ppermute | solution.py:39
  115.5 3.6 %pad_maximum_fusion = bf16[2,4,3,128,1024]{4,3,2,1,0:T(8,128)(2,1)} fusion(bf16[2,2,3,128,1024]{4,3,2,1,0:T(8,128)(2,1)S(1)} %collective-permute-done.3, bf16[2,1,3,128,1024]{4,3,2,1,0:T(8,128)(2,1)S(1)} %collective-permute-done.2, bf16[2,1,1,128,1024]{4,3,2,1,0:T(8,128)(2,1)S(1)} %collective-permute-done.1, bf16[1,1,1,128,1024]{4,3,2,1,0:T(8,128)(2,1)S(1)} %bitcast.58, ...), kind=kLoop, calls=%fused_computation.11 | loop fusion | flops 15728640 | bytes 12582912 | tf_op jit(solution)/shard_map/concatenate | solution.py:38
  120.4 2.8 constant_dynamic-update-slice_fusion.5
  123.2 2.2 constant_dynamic-update-slice_fusion.4
  125.4 131.7 %collective-permute-done.4 = bf16[2,4,3,128,1024]{4,3,2,1,0:T(8,128)(2,1)} collective-permute-done((bf16[2,4,3,128,1024]{4,3,2,1,0:T(8,128)(2,1)}, bf16[2,4,3,128,1024]{4,3,2,1,0:T(8,128)(2,1)}, u32[]{:S(2)}, u32[]{:S(2)}) %collective-permute-start.4) | collective-permute-done | bytes 6291488 | tf_op jit(solution)/shard_map/ppermute | solution.py:39
  257.1 6.4 %constant_dynamic-update-slice_fusion.3 = bf16[2,16,3,128,1024]{4,3,2,1,0:T(8,128)(2,1)} fusion(bf16[2,16,3,128,1024]{4,3,2,1,0:T(8,128)(2,1)} %constant_dynamic-update-slice_fusion.4, bf16[2,4,3,128,1024]{4,3,2,1,0:T(8,128)(2,1)} %collective-permute-done.4), kind=kLoop, calls=%fused_computation.31 | loop fusion | bytes 12582912
  266.1 2.4 constant_dynamic-update-slice_fusion.1
  268.4 6.5 %constant_dynamic-update-slice_fusion = bf16[2,16,3,128,1024]{4,3,2,1,0:T(8,128)(2,1)} fusion(bf16[2,16,3,128,1024]{4,3,2,1,0:T(8,128)(2,1)} %constant_dynamic-update-slice_fusion.1, bf16[2,4,3,128,1024]{4,3,2,1,0:T(8,128)(2,1)} %collective-permute-done.4), kind=kLoop, calls=%fused_computation.28 | loop fusion | bytes 12582912 | tf_op jit(solution)/shard_map/jit(_roll_dynamic)/concatenate | solution.py:43
  275.0 10.6 %constant_dynamic-slice_fusion = bf16[2,8,3,128,1024]{4,3,2,1,0:T(8,128)(2,1)} fusion(bf16[2,16,3,128,1024]{4,3,2,1,0:T(8,128)(2,1)} %constant_dynamic-update-slice_fusion, s32[]{:T(128)S(6)} %select_n.90), kind=kLoop, calls=%fused_computation.59 | loop fusion | bytes 25165828 | tf_op jit(solution)/shard_map/jit(_roll_dynamic)/dynamic_slice | solution.py:43
  285.6 12.2 %gather_fusion = bf16[64,2,64,1024]{3,2,1,0:T(8,128)(2,1)} fusion(bf16[2,48,64,1024]{3,2,1,0:T(8,128)(2,1)} %bitcast.49, s32[1024]{0:T(1024)S(1)} %pad_clamp_fusion), kind=kCustom, calls=%fused_computation | custom fusion | bytes 33554688 | tf_op jit(solution)/shard_map/gather | solution.py:54
  297.8 12.2 %fusion.39 = (bf16[1,64,64,1024]{3,2,0,1:T(8,128)(2,1)}, bf16[1,64,64,1024]{3,2,0,1:T(8,128)(2,1)}) fusion(bf16[2,64,64,1024]{3,2,0,1:T(8,128)(2,1)} %bitcast.50), kind=kLoop, calls=%fused_computation.62 | loop fusion | bytes 33554432 | tf_op jit(solution)/shard_map/slice | solution.py:55
  310.0 8.8 %copy.15 = bf16[512,8,8,128]{3,2,1,0:T(8,128)(2,1)} copy(bf16[512,8,8,128]{3,1,2,0:T(8,128)(2,1)} %bitcast.52) | data formatting | bytes 16777216
  318.7 8.8 %copy.17 = bf16[512,8,8,128]{3,2,1,0:T(8,128)(2,1)} copy(bf16[512,8,8,128]{3,1,2,0:T(8,128)(2,1)} %bitcast.51) | data formatting | bytes 16777216
  327.6 7.2 %bitcast_reduce_fusion = (f32[2,8,64]{2,1,0:T(8,128)S(1)}, f32[2,8,2048,64]{2,3,1,0:T(8,128)S(1)}) fusion(pred[2,2048]{1,0:T(4,128)(4,1)S(1)} %broadcast_compare_fusion, bf16[2,64,8,128]{3,2,1,0:T(8,128)(2,1)S(1)} %bitcast.64, bf16[2,2048,8,128]{3,2,1,0:T(8,128)(2,1)} %bitcast.54), kind=kOutput, calls=%fused_computation.2 | convolution fusion | flops 543161344 | bytes 17047552 | tf_op jit(solution)/shard_map/bqhd,bkhd->bhqk/dot_general | solution.py:58
  334.8 2.1 fusion.5
  336.9 6.6 %fusion.22 = bf16[2,64,8,128]{3,1,2,0:T(8,128)(2,1)S(1)} fusion(bf16[2,2048,8,128]{3,2,1,0:T(8,128)(2,1)} %bitcast.53, f32[2,8,2048,64]{2,3,1,0:T(8,128)S(1)} %get-tuple-element.10, f32[2,8,64]{2,1,0:T(8,128)S(1)} %get-tuple-element.9, pred[2,2048]{1,0:T(4,128)(4,1)S(1)} %broadcast_compare_fusion, f32[2,64,8]{1,2,0:T(8,128)S(1)} %bitcast.65), kind=kOutput, calls=%fused_computation.23 | convolution fusion | flops 545521664 | bytes 17051648 | tf_op jit(solution)/shard_map/bhqk,bkhd->bqhd/dot_general | solution.py:67
  (41 shorter events, 6.6 us)
Async XLA Ops:
  0.0 115.5 %copy-start.9 = (bf16[1,1,128,1024]{3,2,1,0:T(8,128)(2,1)S(1)}, bf16[1,1,128,1024]{3,2,1,0:T(8,128)(2,1)}, u32[]{:S(2)}) copy-start(bf16[1,1,128,1024]{3,2,1,0:T(8,128)(2,1)} %param.6) | copy-start | bytes 786436
  0.0 115.5 %copy-start.8 = (bf16[1,1,128,1024]{3,2,1,0:T(8,128)(2,1)S(1)}, bf16[1,1,128,1024]{3,2,1,0:T(8,128)(2,1)}, u32[]{:S(2)}) copy-start(bf16[1,1,128,1024]{3,2,1,0:T(8,128)(2,1)} %param.7) | copy-start | bytes 786436
  1.1 118.0 %copy-start.6 = (bf16[2,1,1,128,1024]{4,3,2,1,0:T(8,128)(2,1)}, bf16[2,1,1,128,1024]{4,3,2,1,0:T(8,128)(2,1)S(1)}, u32[]{:S(2)}) copy-start(bf16[2,1,1,128,1024]{4,3,2,1,0:T(8,128)(2,1)S(1)} %pad_maximum_fusion.6) | copy-start | bytes 1572868
  1.2 16.1 %collective-permute-start = (bf16[2,1,1,128,1024]{4,3,2,1,0:T(8,128)(2,1)S(1)}, bf16[2,1,1,128,1024]{4,3,2,1,0:T(8,128)(2,1)S(1)}, u32[]{:S(2)}, u32[]{:S(2)}) collective-permute-start(bf16[2,1,1,128,1024]{4,3,2,1,0:T(8,128)(2,1)S(1)} %pad_maximum_fusion.6), channel_id=1, source_target_pairs={{0,1},{1,2},{2,3},{4,5},{5,6},{6,7},{8,9},{9,10},{10,11},{12,13},{... | collective-permute-start | bytes 1572872 | tf_op jit(solution)/shard_map/ppermute | solution.py:20
  6.1 15.3 %collective-permute-start.1 = (bf16[2,1,1,128,1024]{4,3,2,1,0:T(8,128)(2,1)S(1)}, bf16[2,1,1,128,1024]{4,3,2,1,0:T(8,128)(2,1)S(1)}, u32[]{:S(2)}, u32[]{:S(2)}) collective-permute-start(bf16[2,1,1,128,1024]{4,3,2,1,0:T(8,128)(2,1)S(1)} %pad_maximum_fusion.6), channel_id=1, source_target_pairs={{1,0},{2,1},{3,2},{5,4},{6,5},{7,6},{9,8},{10,9},{11,10},{13,12},{... | collective-permute-start | bytes 1572872 | tf_op jit(solution)/shard_map/ppermute | solution.py:22
  17.3 101.9 %copy-start.2 = (bf16[2,1,1,128,1024]{4,3,2,1,0:T(8,128)(2,1)}, bf16[2,1,1,128,1024]{4,3,2,1,0:T(8,128)(2,1)S(1)}, u32[]{:S(2)}) copy-start(bf16[2,1,1,128,1024]{4,3,2,1,0:T(8,128)(2,1)S(1)} %collective-permute-done) | copy-start | bytes 1572868
  21.4 97.8 %copy-start.4 = (bf16[2,1,1,128,1024]{4,3,2,1,0:T(8,128)(2,1)}, bf16[2,1,1,128,1024]{4,3,2,1,0:T(8,128)(2,1)S(1)}, u32[]{:S(2)}) copy-start(bf16[2,1,1,128,1024]{4,3,2,1,0:T(8,128)(2,1)S(1)} %collective-permute-done.1) | copy-start | bytes 1572868
  24.1 95.3 %copy-start.13 = (s32[1,1,2,32]{3,2,1,0:T(2,128)S(1)}, s32[1,1,2,32]{3,2,1,0:T(2,128)}, u32[]{:S(2)}) copy-start(s32[1,1,2,32]{3,2,1,0:T(2,128)} %param.8) | copy-start | bytes 772
  24.1 95.4 %copy-start.10 = (bf16[1,1,128,1024]{3,2,1,0:T(8,128)(2,1)S(1)}, bf16[1,1,128,1024]{3,2,1,0:T(8,128)(2,1)}, u32[]{:S(2)}) copy-start(bf16[1,1,128,1024]{3,2,1,0:T(8,128)(2,1)} %param.5) | copy-start | bytes 786436
  24.1 96.2 %copy-start.12 = (s32[1,1,2]{2,1,0:T(1,128)S(1)}, s32[1,1,2]{2,1,0:T(1,128)}, u32[]{:S(2)}) copy-start(s32[1,1,2]{2,1,0:T(1,128)} %param.9) | copy-start | bytes 28
  24.1 18.6 %collective-permute-start.2 = (bf16[2,1,3,128,1024]{4,3,2,1,0:T(8,128)(2,1)S(1)}, bf16[2,1,3,128,1024]{4,3,2,1,0:T(8,128)(2,1)S(1)}, u32[]{:S(2)}, u32[]{:S(2)}) collective-permute-start(bf16[2,1,3,128,1024]{4,3,2,1,0:T(8,128)(2,1)S(1)} %get-tuple-element.7), channel_id=1, source_target_pairs={{0,28},{4,0},{8,4},{12,8},{16,12},{20,16},{24,20},{28,24},{1,29},{... | collective-permute-start | bytes 4718600 | tf_op jit(solution)/shard_map/ppermute | solution.py:39
  42.7 76.4 %copy-start = (bf16[2,1,3,128,1024]{4,3,2,1,0:T(8,128)(2,1)}, bf16[2,1,3,128,1024]{4,3,2,1,0:T(8,128)(2,1)S(1)}, u32[]{:S(2)}) copy-start(bf16[2,1,3,128,1024]{4,3,2,1,0:T(8,128)(2,1)S(1)} %collective-permute-done.2) | copy-start | bytes 4718596
  44.6 70.9 %collective-permute-start.3 = (bf16[2,2,3,128,1024]{4,3,2,1,0:T(8,128)(2,1)S(1)}, bf16[2,2,3,128,1024]{4,3,2,1,0:T(8,128)(2,1)S(1)}, u32[]{:S(2)}, u32[]{:S(2)}) collective-permute-start(bf16[2,2,3,128,1024]{4,3,2,1,0:T(8,128)(2,1)S(1)} %pad_maximum_fusion.1), channel_id=1, source_target_pairs={{0,24},{4,28},{8,0},{12,4},{16,8},{20,12},{24,16},{28,20},{1,25},{... | collective-permute-start | bytes 9437192 | tf_op jit(solution)/shard_map/ppermute | solution.py:39
  119.2 137.9 %collective-permute-start.4 = (bf16[2,4,3,128,1024]{4,3,2,1,0:T(8,128)(2,1)}, bf16[2,4,3,128,1024]{4,3,2,1,0:T(8,128)(2,1)}, u32[]{:S(2)}, u32[]{:S(2)}) collective-permute-start(bf16[2,4,3,128,1024]{4,3,2,1,0:T(8,128)(2,1)} %pad_maximum_fusion), channel_id=1, source_target_pairs={{0,16},{4,20},{8,24},{12,28},{16,0},{20,4},{24,8},{28,12},{1,17},{... | collective-permute-start | bytes 18874376 | tf_op jit(solution)/shard_map/ppermute | solution.py:39
  123.2 140.3 %copy-start.3 = (bf16[2,1,1,128,1024]{4,3,2,1,0:T(8,128)(2,1)S(1)}, bf16[2,1,1,128,1024]{4,3,2,1,0:T(8,128)(2,1)}, u32[]{:S(2)}) copy-start(bf16[2,1,1,128,1024]{4,3,2,1,0:T(8,128)(2,1)} %copy-done.2) | copy-start | bytes 1572868
  123.2 140.3 %copy-start.5 = (bf16[2,1,1,128,1024]{4,3,2,1,0:T(8,128)(2,1)S(1)}, bf16[2,1,1,128,1024]{4,3,2,1,0:T(8,128)(2,1)}, u32[]{:S(2)}) copy-start(bf16[2,1,1,128,1024]{4,3,2,1,0:T(8,128)(2,1)} %copy-done.4) | copy-start | bytes 1572868
  123.2 140.3 %copy-start.7 = (bf16[2,1,1,128,1024]{4,3,2,1,0:T(8,128)(2,1)S(1)}, bf16[2,1,1,128,1024]{4,3,2,1,0:T(8,128)(2,1)}, u32[]{:S(2)}) copy-start(bf16[2,1,1,128,1024]{4,3,2,1,0:T(8,128)(2,1)} %copy-done.6) | copy-start | bytes 1572868
  125.4 139.4 %copy-start.1 = (bf16[2,1,3,128,1024]{4,3,2,1,0:T(8,128)(2,1)S(1)}, bf16[2,1,3,128,1024]{4,3,2,1,0:T(8,128)(2,1)}, u32[]{:S(2)}) copy-start(bf16[2,1,3,128,1024]{4,3,2,1,0:T(8,128)(2,1)} %copy-done) | copy-start | bytes 4718596
  318.7 8.8 %copy-start.11 = (bf16[16,8,8,128]{3,2,1,0:T(8,128)(2,1)S(1)}, bf16[16,8,8,128]{3,2,1,0:T(8,128)(2,1)}, u32[]{:S(2)}) copy-start(bf16[16,8,8,128]{3,2,1,0:T(8,128)(2,1)} %copy.16) | copy-start | bytes 786436
